TPU v7x, 256 devices: a whole 4x4x8 slice. The times are simulated.
256 devices in a mesh: gx: 8 (over x, core), gy: 32 (over y, z).
Axes of the slice: x: 4, y: 4, z: 8, core: 2. Of those that a mesh axis runs over, the one named last changes fastest.
Arguments:
- hidden_in: bfloat16 [8192, 4096], P('gx', 'gy')
- norm_gain: bfloat16 [4096], P('gy'), may hold values from 0.099609375 to 1.8984375
- query_proj: bfloat16 [4096, 4096], P('gx', 'gy')
- kv_proj: bfloat16 [1024, 4096], P(None, 'gy')
- prompt_lengths: int32 [8], replicated, may hold values from 1 to 4096, 8192 in all
- cache_slot: int32 [512], replicated, may hold values from 0 to 511, as said below
Outputs:
- attention: bfloat16 [8192, 4096], P('gy', 'gx')
- kv_cache: bfloat16 [512, 16, 1024], P('gy', None, 'gx')
Inputs may be any that keep to these rules, and one draw needn't show every extreme that they name: `prompt_lengths`: the 8 prompts sum to 8192 tokens; the longest has exactly 4096. `cache_slot`: A permutation of the 512 slots; slot s is held by index s // 16 of gy. The 16 pages of one token block go to any one index at most 1 times, and every index receives exactly 16 pages.
All inputs are finite; a program needn't handle non-finite values.
Results may differ from a plain program's by a relative error of at most 0.0066.
The roundings to bfloat16 on the way count: a program that leaves them out, or rounds other values in their place, can miss the bound.
Values may be sent and summed in bfloat16 or wider, within the bound.
No kernel may reach another device: no remote copies, remote signals or barrier semaphores. Data moves between devices by JAX's collectives and lax.ppermute only.
A program may use at most 128 MiB of HBM per device.

v0:
```python
import math
import jax
import jax.numpy as jnp
from jax import lax
from jax.sharding import PartitionSpec as P

D = 4096
H = 32
KVH = 4
HD = 128
PAGES_DEV = 16
epsilon = 1e-06
rope_base = 5000000.0
masked_out = -1e30


def token_places(prompt_lengths, token_index):
    prompt_ends = jnp.cumsum(prompt_lengths)
    prompt_starts = prompt_ends - prompt_lengths
    segment = jnp.sum((token_index[:, None] >= prompt_ends[None, :]).astype(jnp.int32), axis=1)
    chosen = segment[:, None] == jnp.arange(prompt_lengths.shape[0], dtype=jnp.int32)[None, :]
    opening = jnp.sum(jnp.where(chosen, prompt_starts[None, :], 0), axis=1)
    return (segment, token_index - opening)


def rotate(vectors, places):
    half_size = vectors.shape[-1] // 2
    frequency = rope_base ** (-(jnp.arange(half_size, dtype=jnp.float32) * 2.0) / vectors.shape[-1])
    angles = places.astype(jnp.float32)[:, None] * frequency[None, :]
    cos_part = jnp.cos(angles)[:, None, :]
    sin_part = jnp.sin(angles)[:, None, :]
    leading = vectors[..., :half_size]
    trailing = vectors[..., half_size:]
    return jnp.concatenate(
        [leading * cos_part - trailing * sin_part, trailing * cos_part + leading * sin_part],
        axis=-1,
    )


def local(hidden_in, norm_gain, query_proj, kv_proj, prompt_lengths, cache_slot):
    count_gx = lax.axis_size("gx")
    count_gy = lax.axis_size("gy")
    where_gx = lax.axis_index("gx")
    where_gy = lax.axis_index("gy")
    local_rows = hidden_in.shape[0]
    block_tokens = local_rows * count_gx // count_gy
    all_tokens = block_tokens * count_gy
    heads_here = query_proj.shape[0] // HD
    group_size = H // KVH
    kv_head = where_gx * heads_here // group_size
    contract = (((1,), (1,)), ((), ()))
    kv_width = 2 * HD
    kv_start = kv_head * 2 * HD
    kv_rows = lax.dynamic_slice_in_dim(kv_proj, kv_start, kv_width, 0)
    widened = hidden_in.astype(jnp.float32)
    squares = jnp.sum(widened * widened, axis=1)
    totals = lax.psum(squares, "gy")
    normed = (
        widened * lax.rsqrt(totals / D + epsilon)[:, None] * norm_gain.astype(jnp.float32)[None, :]
    ).astype(jnp.bfloat16)
    gathered = lax.all_gather(normed, "gx", axis=0, tiled=True)
    stacked = jnp.concatenate([query_proj, kv_rows], axis=0)
    projected = lax.psum_scatter(
        lax.dot_general(gathered, stacked, contract, preferred_element_type=jnp.float32),
        "gy",
        scatter_dimension=0,
        tiled=True,
    )
    every_index = jnp.arange(all_tokens, dtype=jnp.int32)
    segment_all, place_all = token_places(prompt_lengths, every_index)
    first_query = where_gy * block_tokens
    token_index = first_query + jnp.arange(block_tokens, dtype=jnp.int32)
    segment_own = lax.dynamic_slice_in_dim(segment_all, first_query, block_tokens, 0)
    place_own = lax.dynamic_slice_in_dim(place_all, first_query, block_tokens, 0)
    query_cols = heads_here * HD
    queries = rotate(
        projected[:, :query_cols].reshape(block_tokens, heads_here, HD), place_own
    ).astype(jnp.bfloat16)
    keys = rotate(projected[:, query_cols : query_cols + HD][:, None, :], place_own)[
        :, 0, :
    ].astype(jnp.bfloat16)
    values = projected[:, query_cols + HD :].astype(jnp.bfloat16)
    cache_cols = jnp.where(where_gx % 2 == 0, keys, values)
    score_scale = 1.0 / math.sqrt(HD)
    last_query = first_query + block_tokens - 1
    first_segment = segment_own[0]
    initial = (
        jnp.full((heads_here, block_tokens), masked_out, jnp.float32),
        jnp.zeros((heads_here, block_tokens), jnp.float32),
        jnp.zeros((heads_here, block_tokens, HD), jnp.float32),
    )
    key_piece = lax.all_gather(keys, "gy", axis=0, tiled=True)
    value_piece = lax.all_gather(values, "gy", axis=0, tiled=True)
    block_count = key_piece.shape[0] // block_tokens
    key_blocks = key_piece.reshape(block_count, block_tokens, HD)
    value_blocks = value_piece.reshape(block_count, block_tokens, HD)

    def one_block(current, inputs):
        key_rows, value_rows, offset = inputs
        block_begin = offset * block_tokens
        key_segment = lax.dynamic_slice_in_dim(segment_all, block_begin, block_tokens, 0)
        skipped = jnp.logical_or(
            block_begin > last_query, key_segment[block_tokens - 1] < first_segment
        )

        def compute(previous):
            running_max, running_sum, running_acc = previous
            key_index = block_begin + jnp.arange(block_tokens, dtype=jnp.int32)
            allowed = (key_segment[None, :] == segment_own[:, None]) & (
                key_index[None, :] <= token_index[:, None]
            )
            scores = (
                jnp.einsum("qhd,kd->hqk", queries, key_rows, preferred_element_type=jnp.float32)
                * score_scale
            )
            scores = jnp.where(allowed[None], scores, masked_out)
            new_max = jnp.maximum(running_max, jnp.max(scores, axis=2))
            weights = jnp.where(allowed[None], jnp.exp(scores - new_max[..., None]), 0.0)
            factor = jnp.exp(running_max - new_max)
            new_sum = running_sum * factor + jnp.sum(weights, axis=2)
            update = jnp.einsum(
                "hqk,kd->hqd",
                weights.astype(jnp.bfloat16),
                value_rows,
                preferred_element_type=jnp.float32,
            )
            return (new_max, new_sum, running_acc * factor[..., None] + update)

        return (lax.cond(skipped, lambda previous: previous, compute, current), None)

    offsets = jnp.arange(block_count, dtype=jnp.int32)
    result, unused = lax.scan(one_block, initial, (key_blocks, value_blocks, offsets))
    final_max, final_sum, final_acc = result
    attention = (
        (final_acc / final_sum[..., None])
        .transpose(1, 0, 2)
        .reshape(block_tokens, query_cols)
        .astype(jnp.bfloat16)
    )
    pages_dev = PAGES_DEV
    page_len = block_tokens // pages_dev
    width_cols = cache_cols.shape[1]
    my_pages = cache_cols.reshape(pages_dev, page_len * width_cols)
    capacity = max(1, pages_dev // count_gy)
    slots_all = count_gy * capacity
    owners = (cache_slot // pages_dev).reshape(count_gy, pages_dev)
    page_range = jnp.arange(pages_dev, dtype=jnp.int32)
    earlier = page_range[None, :] < page_range[:, None]
    same_owner = owners[:, :, None] == owners[:, None, :]
    ranks = jnp.sum((same_owner & earlier[None]).astype(jnp.int32), axis=2)
    my_owner = lax.dynamic_index_in_dim(owners, where_gy, 0, keepdims=False)
    my_rank = lax.dynamic_index_in_dim(ranks, where_gy, 0, keepdims=False)
    target = my_owner * capacity + my_rank
    slot_range = jnp.arange(slots_all, dtype=jnp.int32)
    send_map = (slot_range[:, None] == target[None, :]).astype(jnp.bfloat16)
    outgoing = jnp.dot(send_map, my_pages, preferred_element_type=jnp.float32).astype(jnp.bfloat16)
    incoming = lax.all_to_all(outgoing, "gy", split_axis=0, concat_axis=0, tiled=True)
    wanted = where_gy * pages_dev + page_range
    matches = cache_slot[None, :] == wanted[:, None]
    page_ids = jnp.arange(cache_slot.shape[0], dtype=jnp.int32)
    source_page = jnp.sum(jnp.where(matches, page_ids[None, :], 0), axis=1)
    source_rank = jnp.sum(jnp.where(matches, ranks.reshape(-1)[None, :], 0), axis=1)
    source_slot = source_page // pages_dev * capacity + source_rank
    take_map = (source_slot[:, None] == slot_range[None, :]).astype(jnp.bfloat16)
    cache_block = jnp.dot(take_map, incoming, preferred_element_type=jnp.float32)
    cache_block = cache_block.astype(jnp.bfloat16).reshape(pages_dev, page_len, width_cols)
    return (attention, cache_block)


def solution(mesh):
    return jax.shard_map(
        local,
        mesh=mesh,
        in_specs=(P("gx", "gy"), P("gy"), P("gx", "gy"), P(None, "gy"), P(), P()),
        out_specs=(P("gy", "gx"), P("gy", None, "gx")),
        check_vma=False,
    )
```

profile of v0, /device:TPU:208, one launch (start us, length us, event | category | flops | bytes accessed | tf_op | source)
XLA Modules:
  0.0 692.0 jit_solution(10577667807313542377)
XLA Ops:
  7.2 1.2 fusion.19
  8.4 58.9 %psum.7 = f32[1024]{0:T(1024)S(1)} all-reduce(f32[1024]{0:T(1024)S(1)} %fusion.19), channel_id=1, replica_groups=mesh['gx'=8,'gy'=32] {'gy'}, use_global_device_ids=true, to_apply=%region_1.2 | all-reduce | flops 1024 | bytes 8192 | tf_op jit(solution)/shard_map/psum | solution.py:57
  67.9 1.9 fusion.21
  69.9 38.3 %all-gather.5.cloned.1.call-done = bf16[8192,128]{1,0:T(8,128)(2,1)} async-done(((bf16[1024,128]{1,0:T(8,128)(2,1)}), bf16[8192,128]{1,0:T(8,128)(2,1)}) %all-gather.5.cloned.1.call-update) | async-done | bytes 2097168 | tf_op jit(solution)/shard_map/all_gather | solution.py:61
  108.2 13.3 %fusion.23 = f32[8192,768]{0,1:T(8,128)} fusion(bf16[8192,128]{1,0:T(8,128)(2,1)} %all-gather.5.cloned.1.call-done, bf16[256,128]{1,0:T(8,128)(2,1)S(1)} %constant_dynamic-slice_fusion, bf16[512,128]{1,0:T(8,128)(2,1)} %param.12), kind=kOutput, calls=%fused_computation.42 | convolution fusion | flops 1611005952 | bytes 27459584 | tf_op jit(solution)/shard_map/dot_general | solution.py:64
  122.8 264.6 %reduce-scatter.2.cloned.1.call-done = f32[256,768]{0,1:T(8,128)} async-done(((f32[8192,768]{0,1:T(8,128)}), f32[256,768]{0,1:T(8,128)}) %reduce-scatter.2.cloned.1.call-update) | async-done | bytes 786448 | tf_op jit(solution)/shard_map/reduce_scatter | solution.py:63
  388.8 1.5 bitcast_select_fusion
  395.8 10.1 %all-to-all-start = ((bf16[32,2,1024]{2,1,0:T(2,128)(2,1)}), bf16[32,2,1024]{2,1,0:T(2,128)(2,1)S(1)}, u32[]{:S(2)}, u32[]{:S(2)}) async-start(bf16[32,2,1024]{2,1,0:T(2,128)(2,1)} %reshape.266), calls=%async_computation.1 | async-start | bytes 262144 | tf_op jit(solution)/shard_map/all_to_all | solution.py:157
  406.2 5.9 all-to-all-done
  413.1 52.7 %all-gather.7.cloned.1.call-done = bf16[8192,128]{0,1:T(8,128)(2,1)} async-done(((bf16[256,128]{0,1:T(8,128)(2,1)}), bf16[8192,128]{0,1:T(8,128)(2,1)}) %all-gather.7.cloned.1.call-update) | async-done | bytes 2097168 | tf_op jit(solution)/shard_map/all_gather | solution.py:93
  465.7 3.2 copy.72
  469.0 72.9 %all-gather.9.cloned.1.call-done = bf16[8192,1,128]{0,2,1:T(8,128)(2,1)} async-done(((bf16[256,1,128]{0,2,1:T(8,128)(2,1)}), bf16[8192,1,128]{0,2,1:T(8,128)(2,1)}) %all-gather.9.cloned.1.call-update) | async-done | bytes 2097168 | tf_op jit(solution)/shard_map/all_gather | solution.py:92
  541.8 4.1 copy.71
  546.0 138.6 %while.15 = (s32[]{:T(128)}, f32[4,256]{1,0:T(4,128)S(1)}, f32[4,256]{1,0:T(4,128)S(1)}, f32[4,256,128]{2,1,0:T(8,128)S(1)}, s32[32]{0:T(128)S(1)}, /*index=5*/s...) while((s32[]{:T(128)}, f32[4,256]{1,0:T(4,128)S(1)}, ...), condition=%wide.region_11.12_spmd.clone, body=%wide.region_6.11_spmd.clone.sunk | while | flops 137038352 | bytes 4926361 | solution.py:132
  568.6 2.1 conditional.3
  573.9 2.1 conditional.3
  574.0 1.2 fusion.46
  579.2 2.1 conditional.3
  584.5 2.1 conditional.3
  589.8 2.1 conditional.3
  595.1 2.1 conditional.3
  600.4 2.1 conditional.3
  605.7 2.1 conditional.3
  611.0 2.1 conditional.3
  616.3 2.1 conditional.3
  621.6 2.1 conditional.3
  626.9 2.1 conditional.3
  632.2 2.1 conditional.3
  637.5 2.1 conditional.3
  642.8 2.1 conditional.3
  648.1 2.1 conditional.3
  653.4 2.1 conditional.3
  (369 shorter events, 85.2 us)
Async XLA Ops:
  7.2 62.7 %copy-start = (bf16[1024,128]{1,0:T(8,128)(2,1)S(1)}, bf16[1024,128]{1,0:T(8,128)(2,1)}, u32[]{:S(2)}) copy-start(bf16[1024,128]{1,0:T(8,128)(2,1)} %param.13) | copy-start | bytes 786436
  7.2 101.1 %all-gather.5.cloned.1.call-start = ((), (), s32[]{:S(2)}) async-start(), calls=%async_computation.2 | async-start | bytes 2359296 | tf_op jit(solution)/shard_map/all_gather | solution.py:61
  69.8 317.6 %reduce-scatter.2.cloned.1.call-start = ((), (), s32[]{:S(2)}) async-start(), calls=%async_computation.3 | async-start | bytes 25952256 | tf_op jit(solution)/shard_map/reduce_scatter | solution.py:63
  121.6 0.7 copy-start.2
  121.6 270.1 %copy-start.1 = (s32[512]{0:T(512)S(1)}, s32[512]{0:T(512)}, u32[]{:S(2)}) copy-start(s32[512]{0:T(512)} %param.15) | copy-start | bytes 6148
  121.6 344.1 %all-gather.7.cloned.1.call-start = ((), (), s32[]{:S(2)}) async-start(), calls=%async_computation.4 | async-start | bytes 2162688 | tf_op jit(solution)/shard_map/all_gather | solution.py:93
  387.5 5.6 slice-start
  390.3 151.5 %all-gather.9.cloned.1.call-start = ((), (), s32[]{:S(2)}) async-start(), calls=%async_computation.5 | async-start | bytes 2162688 | tf_op jit(solution)/shard_map/all_gather | solution.py:92
  395.8 16.3 %all-to-all-start = ((bf16[32,2,1024]{2,1,0:T(2,128)(2,1)}), bf16[32,2,1024]{2,1,0:T(2,128)(2,1)S(1)}, u32[]{:S(2)}, u32[]{:S(2)}) async-start(bf16[32,2,1024]{2,1,0:T(2,128)(2,1)} %reshape.266), calls=%async_computation.1 | async-start | bytes 262144 | tf_op jit(solution)/shard_map/all_to_all | solution.py:157
Sparse Core Ops, SparseCore 0:
  69.9 38.2 all-gather.4
  121.7 265.7 reduce-scatter.1
  390.5 75.2 all-gather.6
  468.1 73.7 all-gather.8
where the time goes:
time: 694 us; the launch traced here: 692 us
  waiting for transfers between devices  434 us (63%)
  loops' own time  63.5 us (9%)
  blocking collectives  58.9 us (8%)
  local copies, waits for them, and re-layouts  52.8 us (8%)
  matrix products  42.2 us (6%)
  other arithmetic  16 us (2%)
  between operations  14 us (2%)
  starting transfers between devices  10.3 us (1%)
    reduce_scatter x1, waiting for transfers between devices, local(): lax.psum_scatter(lax.dot_general(gathered, stacked, contract, preferred_e...  265 us
    all_gather x1, waiting for transfers between devices, local(): key_piece = lax.all_gather(keys, 'gy', axis=0, tiled=True)  72.9 us
    another operation x1, loops' own time, local(): lax.scan(one_block, initial, (key_blocks, value_blocks, offsets))  62.1 us
    psum x1, blocking collectives, local(): totals = lax.psum(squares, 'gy')  58.9 us
    all_gather x1, waiting for transfers between devices, local(): value_piece = lax.all_gather(values, 'gy', axis=0, tiled=True)  52.7 us
    all_gather x1, waiting for transfers between devices, local(): gathered = lax.all_gather(normed, 'gx', axis=0, tiled=True)  38.3 us
    dot_general x17, matrix products, compute(): jnp.einsum('qhd,kd->hqk', queries, key_rows, preferred_element_type=jnp.f...  19.9 us
    slice x32, local copies, waits for them, and re-layouts, one_block(): key_segment[block_tokens - 1] < first_segment  18.9 us
  transfers between devices with their start and end apart: 5, of which 5 were waited for; matrix products, arithmetic and copies ran while one was open for 1% of the time, Pallas kernels for 0%

commit v1 on v0

--- a/solution.py
+++ b/solution.py
@@ -54,7 +54,8 @@
     kv_rows = lax.dynamic_slice_in_dim(kv_proj, kv_start, kv_width, 0)
     widened = hidden_in.astype(jnp.float32)
     squares = jnp.sum(widened * widened, axis=1)
-    totals = lax.psum(squares, "gy")
+    step_on_figure_now = lambda z: jnp.sum(lax.all_gather(z, "gy"), axis=0)
+    totals = step_on_figure_now(squares)
     normed = (
         widened * lax.rsqrt(totals / D + epsilon)[:, None] * norm_gain.astype(jnp.float32)[None, :]
     ).astype(jnp.bfloat16)

time: 694 us -> 667 us (0.961)
  blocking collectives: 58.9 us -> 40.1 us
  waiting for transfers between devices: 434 us -> 426 us
    psum x1 -> x0, blocking collectives: 58.9 us -> none  [local(): totals = lax.psum(squares, 'gy')]
    all_gather x0 -> x1, blocking collectives: none -> 40.1 us  [local(): step_on_figure_now = lambda z: jnp.sum(lax.all_gather(z, 'gy'), axis=0)]
    all_gather x1, waiting for transfers between devices: 38.3 us -> 29.7 us  [local(): gathered = lax.all_gather(normed, 'gx', axis=0, tiled=True)]
  transfers between devices with their start and end apart: 5 -> 5, of which waited for: 5 -> 5; matrix products, arithmetic and copies ran while one was open for 1% -> 2% of each run, Pallas kernels for 0% -> 0%
where the time goes in v1:
time: 667 us; the launch traced here: 665 us
  waiting for transfers between devices  426 us (64%)
  loops' own time  63.5 us (10%)
  local copies, waits for them, and re-layouts  52.8 us (8%)
  matrix products  42.2 us (6%)
  blocking collectives  40.1 us (6%)
  other arithmetic  16 us (2%)
  between operations  14 us (2%)
  starting transfers between devices  10.3 us (2%)
    reduce_scatter x1, waiting for transfers between devices, local(): lax.psum_scatter(lax.dot_general(gathered, stacked, contract, preferred_e...  264 us
    all_gather x1, waiting for transfers between devices, local(): key_piece = lax.all_gather(keys, 'gy', axis=0, tiled=True)  72.9 us
    another operation x1, loops' own time, local(): lax.scan(one_block, initial, (key_blocks, value_blocks, offsets))  62.1 us
    all_gather x1, waiting for transfers between devices, local(): value_piece = lax.all_gather(values, 'gy', axis=0, tiled=True)  52.7 us
    all_gather x1, blocking collectives, local(): step_on_figure_now = lambda z: jnp.sum(lax.all_gather(z, 'gy'), axis=0)  40.1 us
    all_gather x1, waiting for transfers between devices, local(): gathered = lax.all_gather(normed, 'gx', axis=0, tiled=True)  29.7 us
    dot_general x17, matrix products, compute(): jnp.einsum('qhd,kd->hqk', queries, key_rows, preferred_element_type=jnp.f...  19.9 us
    slice x32, local copies, waits for them, and re-layouts, one_block(): key_segment[block_tokens - 1] < first_segment  18.9 us
  transfers between devices with their start and end apart: 5, of which 5 were waited for; matrix products, arithmetic and copies ran while one was open for 2% of the time, Pallas kernels for 0%

profile of v1, /device:TPU:208, one launch (start us, length us, event | category | flops | bytes accessed | tf_op | source)
XLA Modules:
  0.0 664.6 jit_solution(13416813856976006922)
XLA Ops:
  7.2 1.2 fusion.19
  8.4 40.1 %all-gather = f32[32768]{0:T(1024)S(1)} all-gather(f32[1024]{0:T(1024)S(1)} %fusion.19), channel_id=2, replica_groups=mesh['gx'=8,'gy'=32] {'gy'}, dimensions={0}, use_global_device_ids=true | all-gather | bytes 135168 | tf_op jit(solution)/shard_map/all_gather | solution.py:57
  49.3 1.9 fusion.21
  51.2 29.7 %all-gather.6.cloned.1.call-done = bf16[8192,128]{1,0:T(8,128)(2,1)} async-done(((bf16[1024,128]{1,0:T(8,128)(2,1)}), bf16[8192,128]{1,0:T(8,128)(2,1)}) %all-gather.6.cloned.1.call-update) | async-done | bytes 2097168 | tf_op jit(solution)/shard_map/all_gather | solution.py:62
  80.9 13.3 %fusion.23 = f32[8192,768]{0,1:T(8,128)} fusion(bf16[8192,128]{1,0:T(8,128)(2,1)} %all-gather.6.cloned.1.call-done, bf16[256,128]{1,0:T(8,128)(2,1)S(1)} %constant_dynamic-slice_fusion, bf16[512,128]{1,0:T(8,128)(2,1)} %param.12), kind=kOutput, calls=%fused_computation.42 | convolution fusion | flops 1611005952 | bytes 27459584 | tf_op jit(solution)/shard_map/dot_general | solution.py:65
  95.5 264.4 %reduce-scatter.2.cloned.1.call-done = f32[256,768]{0,1:T(8,128)} async-done(((f32[8192,768]{0,1:T(8,128)}), f32[256,768]{0,1:T(8,128)}) %reduce-scatter.2.cloned.1.call-update) | async-done | bytes 786448 | tf_op jit(solution)/shard_map/reduce_scatter | solution.py:64
  361.3 1.5 bitcast_select_fusion
  368.3 10.1 %all-to-all-start = ((bf16[32,2,1024]{2,1,0:T(2,128)(2,1)}), bf16[32,2,1024]{2,1,0:T(2,128)(2,1)S(1)}, u32[]{:S(2)}, u32[]{:S(2)}) async-start(bf16[32,2,1024]{2,1,0:T(2,128)(2,1)} %reshape.271), calls=%async_computation.1 | async-start | bytes 262144 | tf_op jit(solution)/shard_map/all_to_all | solution.py:158
  378.7 5.9 all-to-all-done
  385.6 52.7 %all-gather.8.cloned.1.call-done = bf16[8192,128]{0,1:T(8,128)(2,1)} async-done(((bf16[256,128]{0,1:T(8,128)(2,1)}), bf16[8192,128]{0,1:T(8,128)(2,1)}) %all-gather.8.cloned.1.call-update) | async-done | bytes 2097168 | tf_op jit(solution)/shard_map/all_gather | solution.py:94
  438.3 3.2 copy.72
  441.5 72.9 %all-gather.10.cloned.1.call-done = bf16[8192,1,128]{0,2,1:T(8,128)(2,1)} async-done(((bf16[256,1,128]{0,2,1:T(8,128)(2,1)}), bf16[8192,1,128]{0,2,1:T(8,128)(2,1)}) %all-gather.10.cloned.1.call-update) | async-done | bytes 2097168 | tf_op jit(solution)/shard_map/all_gather | solution.py:93
  514.4 4.1 copy.71
  518.5 138.6 %while.15 = (s32[]{:T(128)}, f32[4,256]{1,0:T(4,128)S(1)}, f32[4,256]{1,0:T(4,128)S(1)}, f32[4,256,128]{2,1,0:T(8,128)S(1)}, s32[32]{0:T(128)S(1)}, /*index=5*/s...) while((s32[]{:T(128)}, f32[4,256]{1,0:T(4,128)S(1)}, ...), condition=%wide.region_11.12_spmd.clone, body=%wide.region_6.11_spmd.clone.sunk | while | flops 137038352 | bytes 4926361 | solution.py:133
  541.1 2.1 conditional.3
  541.2 1.2 fusion.46
  546.4 2.1 conditional.3
  551.7 2.1 conditional.3
  557.0 2.1 conditional.3
  562.3 2.1 conditional.3
  567.6 2.1 conditional.3
  572.9 2.1 conditional.3
  578.2 2.1 conditional.3
  583.5 2.1 conditional.3
  588.8 2.1 conditional.3
  594.1 2.1 conditional.3
  599.4 2.1 conditional.3
  604.7 2.1 conditional.3
  610.0 2.1 conditional.3
  615.3 2.1 conditional.3
  620.6 2.1 conditional.3
  625.9 2.1 conditional.3
  (371 shorter events, 85.3 us)
Async XLA Ops:
  7.2 44.1 %copy-start = (bf16[1024,128]{1,0:T(8,128)(2,1)S(1)}, bf16[1024,128]{1,0:T(8,128)(2,1)}, u32[]{:S(2)}) copy-start(bf16[1024,128]{1,0:T(8,128)(2,1)} %param.13) | copy-start | bytes 786436
  7.2 73.7 %all-gather.6.cloned.1.call-start = ((), (), s32[]{:S(2)}) async-start(), calls=%async_computation.2 | async-start | bytes 2359296 | tf_op jit(solution)/shard_map/all_gather | solution.py:62
  51.1 308.8 %reduce-scatter.2.cloned.1.call-start = ((), (), s32[]{:S(2)}) async-start(), calls=%async_computation.3 | async-start | bytes 25952256 | tf_op jit(solution)/shard_map/reduce_scatter | solution.py:64
  94.3 0.7 copy-start.2
  94.3 269.9 %copy-start.1 = (s32[512]{0:T(512)S(1)}, s32[512]{0:T(512)}, u32[]{:S(2)}) copy-start(s32[512]{0:T(512)} %param.15) | copy-start | bytes 6148
  94.3 344.0 %all-gather.8.cloned.1.call-start = ((), (), s32[]{:S(2)}) async-start(), calls=%async_computation.4 | async-start | bytes 2162688 | tf_op jit(solution)/shard_map/all_gather | solution.py:94
  360.0 5.6 slice-start
  362.8 151.5 %all-gather.10.cloned.1.call-start = ((), (), s32[]{:S(2)}) async-start(), calls=%async_computation.5 | async-start | bytes 2162688 | tf_op jit(solution)/shard_map/all_gather | solution.py:93
  368.3 16.3 %all-to-all-start = ((bf16[32,2,1024]{2,1,0:T(2,128)(2,1)}), bf16[32,2,1024]{2,1,0:T(2,128)(2,1)S(1)}, u32[]{:S(2)}, u32[]{:S(2)}) async-start(bf16[32,2,1024]{2,1,0:T(2,128)(2,1)} %reshape.271), calls=%async_computation.1 | async-start | bytes 262144 | tf_op jit(solution)/shard_map/all_to_all | solution.py:158
Sparse Core Ops, SparseCore 0:
  51.3 29.6 all-gather.5
  94.4 265.5 reduce-scatter.1
  362.9 75.2 all-gather.7
  440.6 73.7 all-gather.9
